TPU v7x, 128 devices: a whole 4x4x4 slice. The times are simulated.
128 devices in a mesh: dp: 32 (over y, z_lo, x), tensor: 4 (over z_hi, core).
Axes of the slice: x: 4, y: 4, z: 4 (z_hi: 2, z_lo: 2; z = z_hi * 2 + z_lo), core: 2. Of those that a mesh axis runs over, the one named last changes fastest.
Arguments:
- tokens: bfloat16 [32768, 4096], P('dp'), may hold values from -6 to 6
- grad_out: bfloat16 [32768, 2048], P('dp', 'tensor'), may hold values from -12 to 12
- w_query: bfloat16 [4096, 2048], P('dp', 'tensor'), may hold values from -2 to 2
- w_key: bfloat16 [4096, 512], P('dp', 'tensor'), may hold values from -2 to 2
- value_matrix: bfloat16 [4096, 512], P('dp', 'tensor'), may hold values from -0.09375 to 0.09375
Outputs:
- grad_tokens: bfloat16 [32768, 4096], P('dp', 'tensor')
- grad_query: bfloat16 [4096, 2048], P('dp', 'tensor')
- grad_key: bfloat16 [4096, 512], P('dp', 'tensor')
- grad_value: bfloat16 [4096, 512], P('dp', 'tensor')
All inputs are finite; a program needn't handle non-finite values.
Results may differ from a plain program's by a relative error of at most 0.03.
The roundings to bfloat16 on the way count: a program that leaves them out, or rounds other values in their place, can miss the bound.
Values may be sent and summed in bfloat16 or wider, within the bound.
No kernel may reach another device: no remote copies, remote signals or barrier semaphores. Data moves between devices by JAX's collectives and lax.ppermute only.
A program may use at most 192 MiB of HBM per device.

v0:
```python
import jax
import jax.numpy as jnp
from jax import lax
from jax.sharding import PartitionSpec as P

MODEL_WIDTH = 4096
HEAD_SIZE = 128
rope_base = 500000.0


def position_tables(length, head_dim):
    half_dim = head_dim // 2
    positions = jnp.arange(length, dtype=jnp.float32)
    inverse = jnp.power(
        jnp.float32(rope_base), -2.0 * jnp.arange(half_dim, dtype=jnp.float32) / head_dim
    )
    angles = positions[:, None] * inverse[None, :]
    cosine = jnp.concatenate([jnp.cos(angles), jnp.cos(angles)], axis=-1)[:, None, :]
    sine_table = jnp.concatenate([jnp.sin(angles), jnp.sin(angles)], axis=-1)[:, None, :]
    return (cosine, sine_table)


def half_turn(values):
    lower, upper = jnp.split(values, 2, axis=-1)
    return jnp.concatenate([-upper, lower], axis=-1)


def rotate_forward(values, cosine, sine_table):
    return values * cosine + half_turn(values) * sine_table


def rotate_back(grads, cosine, sine_table):
    return grads * cosine - half_turn(grads * sine_table)


def attention_backward(unrotated_query, unrotated_key, projected_value, upstream_flat, kv_heads):
    length = unrotated_query.shape[0]
    heads = unrotated_query.shape[1] // HEAD_SIZE
    group_size = heads // kv_heads
    cosine, sine_table = position_tables(length, HEAD_SIZE)
    query = rotate_forward(
        unrotated_query.reshape(length, heads, HEAD_SIZE), cosine, sine_table
    ).astype(jnp.bfloat16)
    key = rotate_forward(
        unrotated_key.reshape(length, kv_heads, HEAD_SIZE), cosine, sine_table
    ).astype(jnp.bfloat16)
    value = projected_value.reshape(length, kv_heads, HEAD_SIZE).astype(jnp.bfloat16)
    query_grouped = query.reshape(length, kv_heads, group_size, HEAD_SIZE)
    upstream = upstream_flat.reshape(length, kv_heads, group_size, HEAD_SIZE)
    scale = 1.0 / jnp.sqrt(jnp.float32(HEAD_SIZE))
    scores = (
        jnp.einsum("ikgd,jkd->kgij", query_grouped, key, preferred_element_type=jnp.float32) * scale
    )
    positions = jnp.arange(length, dtype=jnp.int32)
    causal = positions[:, None] >= positions[None, :]
    scores = jnp.where(causal, scores, -jnp.inf)
    row_max = jnp.max(scores, axis=-1, keepdims=True)
    weights = jnp.exp(scores - row_max)
    weights = weights / jnp.sum(weights, axis=-1, keepdims=True)
    weights_b = weights.astype(jnp.bfloat16)
    dprob = jnp.einsum("ikgd,jkd->kgij", upstream, value, preferred_element_type=jnp.float32)
    rowdot = jnp.sum(weights * dprob, axis=-1, keepdims=True)
    dscore = (weights * (dprob - rowdot) * scale).astype(jnp.bfloat16)
    dquery = jnp.einsum("kgij,jkd->ikgd", dscore, key, preferred_element_type=jnp.float32).reshape(
        length, heads, HEAD_SIZE
    )
    dkey = jnp.einsum("kgij,ikgd->jkd", dscore, query_grouped, preferred_element_type=jnp.float32)
    dvalue = jnp.einsum("kgij,ikgd->jkd", weights_b, upstream, preferred_element_type=jnp.float32)
    query_gradient = (
        rotate_back(dquery, cosine, sine_table)
        .astype(jnp.bfloat16)
        .reshape(length, heads * HEAD_SIZE)
    )
    key_gradient = (
        rotate_back(dkey, cosine, sine_table)
        .astype(jnp.bfloat16)
        .reshape(length, kv_heads * HEAD_SIZE)
    )
    value_gradient = dvalue.astype(jnp.bfloat16).reshape(length, kv_heads * HEAD_SIZE)
    return (query_gradient, key_gradient, value_gradient)


def contract_cols(grads, weight_rows):
    return lax.dot_general(
        grads, weight_rows, (((1,), (1,)), ((), ())), preferred_element_type=jnp.float32
    )


def body(tokens, grad_out, w_query, w_key, value_matrix):
    query_cols = w_query.shape[1]
    key_value_columns = w_key.shape[1]
    kv_dev = key_value_columns // HEAD_SIZE
    pieces = (
        lax.all_gather(w_query, "dp", axis=0, tiled=True),
        lax.all_gather(w_key, "dp", axis=0, tiled=True),
        lax.all_gather(value_matrix, "dp", axis=0, tiled=True),
    )
    unrotated_query, unrotated_key, projected_value = tuple(
        (jnp.dot(tokens, piece, preferred_element_type=jnp.float32) for piece in pieces)
    )
    query_gradient, key_gradient, value_gradient = attention_backward(
        unrotated_query, unrotated_key, projected_value, grad_out, kv_dev
    )
    combined = jnp.concatenate([query_gradient, key_gradient, value_gradient], axis=1)
    pieces = lax.all_gather((w_query, w_key, value_matrix), "dp", axis=0, tiled=True)
    partial_sum = (
        contract_cols(query_gradient, pieces[0])
        + contract_cols(key_gradient, pieces[1])
        + contract_cols(value_gradient, pieces[2])
    )
    summed_all = lax.psum(partial_sum.astype(jnp.bfloat16), "tensor").astype(jnp.float32)
    share_width = MODEL_WIDTH // lax.axis_size("tensor")
    grad_tokens = lax.dynamic_slice_in_dim(
        summed_all, lax.axis_index("tensor") * share_width, share_width, 1
    )
    grads_all = lax.psum_scatter(
        lax.dot_general(
            tokens, combined, (((0,), (0,)), ((), ())), preferred_element_type=jnp.float32
        ).astype(jnp.bfloat16),
        "dp",
        scatter_dimension=0,
        tiled=True,
    ).astype(jnp.float32)
    grad_query = grads_all[:, :query_cols].astype(jnp.bfloat16)
    grad_key = grads_all[:, query_cols : query_cols + key_value_columns].astype(jnp.bfloat16)
    grad_value = grads_all[:, query_cols + key_value_columns :].astype(jnp.bfloat16)
    return (grad_tokens.astype(jnp.bfloat16), grad_query, grad_key, grad_value)


def solution(mesh):
    in_specs = (
        P("dp", None),
        P("dp", "tensor"),
        P("dp", "tensor"),
        P("dp", "tensor"),
        P("dp", "tensor"),
    )
    out_specs = (P("dp", "tensor"), P("dp", "tensor"), P("dp", "tensor"), P("dp", "tensor"))
    return jax.shard_map(body, mesh=mesh, in_specs=in_specs, out_specs=out_specs, check_vma=False)
```

profile of v0, /device:TPU:0, one launch (start us, length us, event | category | flops | bytes accessed | tf_op | source)
XLA Modules:
  0.0 889.6 jit_solution(15293957988102845399)
XLA Ops:
  7.2 0.0 all-gather.4.cloned.1.call-start
  7.2 0.7 all-gather.4.cloned.1.call-update
  7.9 0.0 all-gather.6.cloned.1.call-start
  7.9 0.7 all-gather.6.cloned.1.call-update
  8.6 0.0 all-gather.8.cloned.1.call-start
  8.7 0.7 all-gather.8.cloned.1.call-update
  9.4 0.0 all-reduce.2.cloned.1.call-start
  9.4 0.3 iota_compare_fusion
  9.8 1.0 fusion.38
  10.8 0.0 copy-start.10
  10.8 2.4 copy.40
  13.1 149.9 %all-gather.4.cloned.1.call-done = bf16[4096,128]{1,0:T(8,128)(2,1)} async-done(((bf16[128,128]{1,0:T(8,128)(2,1)}), bf16[4096,128]{1,0:T(8,128)(2,1)}) %all-gather.4.cloned.1.call-update) | async-done | bytes 1048592 | tf_op jit(solution)/shard_map/all_gather | solution.py:95
  163.1 6.5 fusion.43
  169.6 1.2 pad_maximum_fusion.1
  170.8 151.1 %all-gather.6.cloned.1.call-done = bf16[4096,512]{1,0:T(8,128)(2,1)} async-done(((bf16[128,512]{1,0:T(8,128)(2,1)}), bf16[4096,512]{1,0:T(8,128)(2,1)}) %all-gather.6.cloned.1.call-update) | async-done | bytes 4194320 | tf_op jit(solution)/shard_map/all_gather | solution.py:94
  321.9 8.3 fusion.44
  330.2 0.2 slice_negate_fusion.1
  330.4 0.2 maximum_multiply_fusion
  330.6 0.0 copy-start.1
  330.6 0.6 copy-done.3
  331.2 0.6 fusion.14
  331.8 0.1 copy-done.1
  331.9 3.1 fusion.6
  335.1 3.6 fusion.5
  338.7 2.3 copy-done
  341.0 6.0 fusion.25
  347.0 127.4 %all-gather.8.cloned.1.call-done = bf16[4096,128]{1,0:T(8,128)(2,1)} async-done(((bf16[128,128]{1,0:T(8,128)(2,1)}), bf16[4096,128]{1,0:T(8,128)(2,1)}) %all-gather.8.cloned.1.call-update) | async-done | bytes 1048592 | tf_op jit(solution)/shard_map/all_gather | solution.py:96
  474.4 18.2 %fusion = (f32[4,1024]{1,0:T(4,128)S(1)}, f32[1024,1024,4]{1,0,2:T(8,128)}) fusion(f32[4,1024]{1,0:T(4,128)S(1)} %fusion.5, f32[4,1024]{1,0:T(4,128)S(1)} %get-tuple-element.27, f32[1024,1024,4]{1,0,2:T(8,128)} %copy-done, pred[1024,1024]{0,1:T(8,128)(4,1)S(1)} %iota_compare_fusion, bf16[1024,4,128]{0,2,1:T(8,128)(2,1)} %bitcast.132, ...), kind=kOutput, calls=%fused_computation.3 | convolution fusion | flops 2172776448 | bytes 45137920 | tf_op jit(solution)/shard_map/ikgd,jkd->kgij/dot_general | solution.py:61
  492.7 13.4 %fusion.7 = bf16[4,1024,1024]{1,2,0:T(8,128)(2,1)S(1)} fusion(f32[1024,1024,4]{1,0,2:T(8,128)} %get-tuple-element.30, f32[4,1024]{1,0:T(4,128)S(1)} %get-tuple-element.29, f32[4,1024]{1,0:T(4,128)S(1)} %fusion.5, f32[4,1024]{1,0:T(4,128)S(1)} %get-tuple-element.27, f32[1024,1024,4]{1,0,2:T(8,128)} %copy-done, pred[1024,1024]{0,1:T(8,128)(4,1)S(1)} %iota_compare_fusion), kind=kLoop, calls=%fused_computation.12 | loop fusion | flops 33554432 | bytes 43040768 | tf_op jit(solution)/shard_map/reshape.19
  506.1 3.0 bitcast_multiply_fusion.4
  509.1 1.4 bitcast_multiply_fusion.3
  510.5 0.3 slice_negate_fusion
  510.8 0.2 pad_maximum_fusion
  511.0 0.6 fusion.16
  511.7 0.1 fusion.34
  511.8 8.1 fusion.46
  519.9 8.1 fusion.45
  528.0 15.3 %add_convert_fusion = bf16[1024,4096]{1,0:T(8,128)(2,1)} fusion(f32[1024,4096]{1,0:T(8,128)} %fusion.45, f32[1024,4096]{1,0:T(8,128)} %fusion.46, bf16[1024,128]{0,1:T(8,128)(2,1)S(1)} %copy-done.14, bf16[4096,128]{1,0:T(8,128)(2,1)S(1)} %copy-done.13), kind=kOutput, calls=%fused_computation.7 | convolution fusion | flops 1086324736 | bytes 43253760 | tf_op jit(solution)/shard_map/dot_general | solution.py:84
  543.4 0.0 all-reduce.2.cloned.1.call-update
  543.4 0.0 reduce-scatter.4.cloned.1.call-start
  543.4 13.3 %fusion.11 = bf16[4096,768]{0,1:T(8,128)(2,1)} fusion(bf16[1024,4096]{1,0:T(8,128)(2,1)} %param.5, bf16[1024,128]{0,1:T(8,128)(2,1)S(1)} %copy-done.14, bf16[1024,128]{0,1:T(8,128)(2,1)S(1)} %fusion.34, bf16[1024,512]{0,1:T(8,128)(2,1)S(1)} %fusion.16), kind=kOutput, calls=%fused_computation.17 | convolution fusion | flops 6450315264 | bytes 16252928 | tf_op jit(solution)/shard_map/dot_general | solution.py:117
  556.7 8.5 copy.35
  565.2 0.0 reduce-scatter.4.cloned.1.call-update
  565.2 138.8 %all-reduce.2.cloned.1.call-done = bf16[1024,4096]{1,0:T(8,128)(2,1)} async-done(((bf16[1024,4096]{1,0:T(8,128)(2,1)}), bf16[1024,4096]{1,0:T(8,128)(2,1)}) %all-reduce.2.cloned.1.call-update) | async-done | bytes 8388624 | tf_op jit(solution)/shard_map/psum | solution.py:111
  704.0 3.1 convert_convert_fusion
  707.1 173.1 %reduce-scatter.4.cloned.1.call-done = bf16[128,768]{1,0:T(8,128)(2,1)} async-done(((bf16[4096,768]{1,0:T(8,128)(2,1)}), bf16[128,768]{1,0:T(8,128)(2,1)}) %reduce-scatter.4.cloned.1.call-update) | async-done | bytes 196624
  880.1 1.6 slice.15
  881.7 1.4 fusion.42
  (30 shorter events, 0.1 us)
Async XLA Ops:
  7.2 155.9 %all-gather.4.cloned.1.call-start = ((), (), s32[]{:S(2)}) async-start(), calls=%async_computation.1 | async-start | bytes 1081344 | tf_op jit(solution)/shard_map/all_gather | solution.py:95
  7.9 314.0 %all-gather.6.cloned.1.call-start = ((), (), s32[]{:S(2)}) async-start(), calls=%async_computation.2 | async-start | bytes 4325376 | tf_op jit(solution)/shard_map/all_gather | solution.py:94
  8.6 465.8 %all-gather.8.cloned.1.call-start = ((), (), s32[]{:S(2)}) async-start(), calls=%async_computation.3 | async-start | bytes 1081344 | tf_op jit(solution)/shard_map/all_gather | solution.py:96
  9.4 694.6 %all-reduce.2.cloned.1.call-start = ((), (), s32[]{:S(2)}) async-start(), calls=%async_computation.4 | async-start | bytes 16777216 | tf_op jit(solution)/shard_map/psum | solution.py:111
  10.8 158.9 %copy-start.10 = (f32[1024,64]{0,1:T(8,128)}, f32[1024,64]{0,1:T(8,128)S(1)}, u32[]{:S(2)}) copy-start(f32[1024,64]{0,1:T(8,128)S(1)} %get-tuple-element.25) | copy-start | bytes 786436
  321.9 8.5 copy-start.5
  330.2 1.0 copy-start.3
  330.2 1.7 copy-start.8
  330.6 1.3 copy-start.1
  335.0 5.9 copy-start
  335.1 5.9 copy-start.12
  492.6 13.4 %copy-start.2 = (f32[1024,4,128]{0,2,1:T(8,128)S(1)}, f32[1024,4,128]{0,2,1:T(8,128)}, u32[]{:S(2)}) copy-start(f32[1024,4,128]{0,2,1:T(8,128)} %copy-done.1) | copy-start | bytes 6291460
  492.7 13.4 %copy-start.4 = (f32[1024,128]{0,1:T(8,128)S(1)}, f32[1024,128]{0,1:T(8,128)}, u32[]{:S(2)}) copy-start(f32[1024,128]{0,1:T(8,128)} %get-tuple-element.20) | copy-start | bytes 1572868
  506.1 3.0 copy-start.6
  506.1 3.0 copy-start.9
  510.5 1.2 copy-start.11
  510.5 1.3 copy-start.7
  511.8 8.1 copy-start.15
  519.9 8.1 copy-start.13
  519.9 8.1 copy-start.14
  543.4 336.8 %reduce-scatter.4.cloned.1.call-start = ((), (), s32[]{:S(2)}) async-start(), calls=%async_computation.5 | async-start | bytes 6488064
Sparse Core Ops, SparseCore 0:
  9.6 153.3 all-gather.3
  164.7 157.1 all-gather.5
  323.5 150.8 all-gather.7
  543.5 160.4 all-reduce.1
  706.3 173.8 reduce-scatter.3
where the time goes:
time: 890 us
  waiting for transfers between devices  742 us (83%)
  matrix products  91.3 us (10%)
  other arithmetic  24.8 us (3%)
  local copies, waits for them, and re-layouts  16.8 us (2%)
  between operations  14.1 us (2%)
    unnamed x6, waiting for transfers between devices  175 us
    all_gather x1, waiting for transfers between devices, body(): lax.all_gather(w_query, 'dp', axis=0, tiled=True)  151 us
    all_gather x1, waiting for transfers between devices, body(): lax.all_gather(w_key, 'dp', axis=0, tiled=True)  150 us
    psum x1, waiting for transfers between devices, body(): lax.psum(partial_sum.astype(jnp.bfloat16), 'tensor').astype(jnp.float32)  139 us
    all_gather x1, waiting for transfers between devices, body(): lax.all_gather(value_matrix, 'dp', axis=0, tiled=True)  127 us
    dot_general x3, matrix products, contract_cols(): lax.dot_general(grads, weight_rows, (((1,), (1,)), ((), ())), preferred_e...  31.5 us
    dot_general x1, matrix products, attention_backward(): jnp.einsum('ikgd,jkd->kgij', upstream, value, preferred_element_type=jnp....  18.2 us
  transfers between devices with their start and end apart: 5, of which 5 were waited for; matrix products, arithmetic and copies ran while one was open for 7% of the time, Pallas kernels for 0%

commit v1 on v0

--- a/solution.py
+++ b/solution.py
@@ -93,7 +93,9 @@
     pieces = (
         lax.all_gather(w_query, "dp", axis=0, tiled=True),
         lax.all_gather(w_key, "dp", axis=0, tiled=True),
-        lax.all_gather(value_matrix, "dp", axis=0, tiled=True),
+        jnp.concatenate(
+            lax.all_to_all(jnp.stack([value_matrix] * lax.axis_size("dp")), "dp", 0, 0), axis=0
+        ),
     )
     unrotated_query, unrotated_key, projected_value = tuple(
         (jnp.dot(tokens, piece, preferred_element_type=jnp.float32) for piece in pieces)

time: 890 us -> 839 us (0.943)
  waiting for transfers between devices: 742 us -> 676 us
    all_gather x1, waiting for transfers between devices: 127 us -> 69.6 us  [body(): lax.all_gather((w_query, w_key, value_matrix), 'dp', axis=0, tiled=True)]
    all_gather x1, waiting for transfers between devices: 150 us -> 140 us  [body(): lax.all_gather(w_key, 'dp', axis=0, tiled=True)]
  transfers between devices with their start and end apart: 5 -> 6, of which waited for: 5 -> 5; matrix products, arithmetic and copies ran while one was open for 7% -> 14% of each run, Pallas kernels for 0% -> 0%
where the time goes in v1:
time: 839 us; the launch traced here: 838 us
  waiting for transfers between devices  676 us (81%)
  matrix products  92.4 us (11%)
  other arithmetic  24.6 us (3%)
  local copies, waits for them, and re-layouts  22.5 us (3%)
  between operations  14.1 us (2%)
  starting transfers between devices  9.08 us (1%)
    unnamed x6, waiting for transfers between devices  175 us
    all_gather x1, waiting for transfers between devices, body(): lax.all_gather(w_query, 'dp', axis=0, tiled=True)  152 us
    all_gather x1, waiting for transfers between devices, body(): lax.all_gather(w_key, 'dp', axis=0, tiled=True)  140 us
    psum x1, waiting for transfers between devices, body(): lax.psum(partial_sum.astype(jnp.bfloat16), 'tensor').astype(jnp.float32)  139 us
    all_gather x1, waiting for transfers between devices, body(): lax.all_gather((w_query, w_key, value_matrix), 'dp', axis=0, tiled=True)  69.6 us
    dot_general x3, matrix products, contract_cols(): lax.dot_general(grads, weight_rows, (((1,), (1,)), ((), ())), preferred_e...  33.5 us
    dot_general x1, matrix products, attention_backward(): jnp.einsum('ikgd,jkd->kgij', upstream, value, preferred_element_type=jnp....  18.4 us
  transfers between devices with their start and end apart: 6, of which 5 were waited for; matrix products, arithmetic and copies ran while one was open for 14% of the time, Pallas kernels for 0%

profile of v1, /device:TPU:0, one launch (start us, length us, event | category | flops | bytes accessed | tf_op | source)
XLA Modules:
  0.0 838.3 jit_solution(16931385308182861579)
XLA Ops:
  7.2 0.0 all-gather.4.cloned.1.call-start
  7.2 0.7 all-gather.4.cloned.1.call-update
  7.9 0.0 all-gather.6.cloned.1.call-start
  7.9 0.7 all-gather.6.cloned.1.call-update
  8.6 2.0 stack.2
  10.6 8.9 %all-to-all-start = ((bf16[32,128,128]{2,1,0:T(8,128)(2,1)}), bf16[32,128,128]{2,1,0:T(8,128)(2,1)}, u32[]{:S(2)}, u32[]{:S(2)}) async-start(bf16[32,128,128]{2,1,0:T(8,128)(2,1)} %stack.2), calls=%async_computation | async-start | bytes 2097152 | tf_op jit(solution)/shard_map/all_to_all | solution.py:97
  19.5 0.0 all-gather.8.cloned.1.call-start
  19.6 0.7 all-gather.8.cloned.1.call-update
  20.2 0.0 all-reduce.2.cloned.1.call-start
  20.3 0.3 iota_compare_fusion
  20.6 1.0 fusion.38
  21.6 2.4 copy.40
  24.0 139.9 %all-gather.4.cloned.1.call-done = bf16[4096,128]{1,0:T(8,128)(2,1)} async-done(((bf16[128,128]{1,0:T(8,128)(2,1)}), bf16[4096,128]{1,0:T(8,128)(2,1)}) %all-gather.4.cloned.1.call-update) | async-done | bytes 1048592 | tf_op jit(solution)/shard_map/all_gather | solution.py:95
  163.9 6.5 fusion.43
  170.5 1.2 pad_maximum_fusion.1
  171.7 152.1 %all-gather.6.cloned.1.call-done = bf16[4096,512]{1,0:T(8,128)(2,1)} async-done(((bf16[128,512]{1,0:T(8,128)(2,1)}), bf16[4096,512]{1,0:T(8,128)(2,1)}) %all-gather.6.cloned.1.call-update) | async-done | bytes 4194320 | tf_op jit(solution)/shard_map/all_gather | solution.py:94
  323.8 8.3 fusion.44
  332.1 0.2 slice_negate_fusion.1
  332.2 0.2 maximum_multiply_fusion
  332.5 0.6 copy-done.3
  333.1 0.6 fusion.14
  333.7 0.1 copy-done.1
  333.8 3.1 fusion.6
  336.9 5.7 copy-done
  342.6 3.6 fusion.5
  346.3 18.4 %fusion = (f32[4,1024]{1,0:T(4,128)S(1)}, f32[1024,1024,4]{1,0,2:T(8,128)}) fusion(f32[4,1024]{1,0:T(4,128)S(1)} %fusion.5, f32[4,1024]{1,0:T(4,128)S(1)} %get-tuple-element.27, f32[1024,1024,4]{1,0,2:T(8,128)} %copy-done, pred[1024,1024]{0,1:T(8,128)(4,1)S(1)} %iota_compare_fusion, bf16[1024,4,128]{0,2,1:T(8,128)(2,1)} %bitcast.135, ...), kind=kOutput, calls=%fused_computation.3 | convolution fusion | flops 2172776448 | bytes 45137920 | tf_op jit(solution)/shard_map/ikgd,jkd->kgij/dot_general | solution.py:61
  364.7 13.2 %fusion.7 = bf16[4,1024,1024]{1,2,0:T(8,128)(2,1)S(1)} fusion(f32[1024,1024,4]{1,0,2:T(8,128)} %get-tuple-element.30, f32[4,1024]{1,0:T(4,128)S(1)} %get-tuple-element.29, f32[4,1024]{1,0:T(4,128)S(1)} %fusion.5, f32[4,1024]{1,0:T(4,128)S(1)} %get-tuple-element.27, f32[1024,1024,4]{1,0,2:T(8,128)} %copy-done, pred[1024,1024]{0,1:T(8,128)(4,1)S(1)} %iota_compare_fusion), kind=kLoop, calls=%fused_computation.12 | loop fusion | flops 33554432 | bytes 43040768 | tf_op jit(solution)/shard_map/reshape.21
  378.0 3.0 bitcast_multiply_fusion.4
  381.0 1.4 bitcast_multiply_fusion.3
  382.4 0.3 slice_negate_fusion
  382.7 0.2 pad_maximum_fusion
  382.9 0.6 fusion.16
  383.6 0.1 fusion.34
  383.8 9.4 %fusion.46 = f32[1024,4096]{1,0:T(8,128)} fusion(bf16[1024,128]{0,1:T(8,128)(2,1)S(1)} %fusion.34, bf16[4096,128]{1,0:T(8,128)(2,1)S(1)} %copy-done.7), kind=kOutput, calls=%fused_computation.70 | convolution fusion | flops 1073741824 | bytes 18087936 | tf_op jit(solution)/shard_map/dot_general | solution.py:84
  393.2 8.4 fusion.45
  401.6 5.2 fusion.25
  406.8 69.6 %all-gather.8.cloned.1.call-done = bf16[4096,128]{1,0:T(8,128)(2,1)} async-done(((bf16[128,128]{1,0:T(8,128)(2,1)}), bf16[4096,128]{1,0:T(8,128)(2,1)}) %all-gather.8.cloned.1.call-update) | async-done | bytes 1048592 | tf_op jit(solution)/shard_map/all_gather | solution.py:107
  476.4 15.7 %add_convert_fusion = bf16[1024,4096]{1,0:T(8,128)(2,1)} fusion(f32[1024,4096]{1,0:T(8,128)} %fusion.45, f32[1024,4096]{1,0:T(8,128)} %fusion.46, bf16[1024,128]{0,1:T(8,128)(2,1)S(1)} %fusion.25, bf16[4096,128]{1,0:T(8,128)(2,1)} %all-gather.8.cloned.1.call-done), kind=kOutput, calls=%fused_computation.7 | convolution fusion | flops 1086324736 | bytes 43253760 | tf_op jit(solution)/shard_map/dot_general | solution.py:84
  492.1 0.0 all-reduce.2.cloned.1.call-update
  492.1 0.0 reduce-scatter.4.cloned.1.call-start
  492.1 13.1 %fusion.11 = bf16[4096,768]{0,1:T(8,128)(2,1)} fusion(bf16[1024,4096]{1,0:T(8,128)(2,1)} %param.5, bf16[1024,128]{0,1:T(8,128)(2,1)S(1)} %fusion.25, bf16[1024,128]{0,1:T(8,128)(2,1)S(1)} %fusion.34, bf16[1024,512]{0,1:T(8,128)(2,1)S(1)} %fusion.16), kind=kOutput, calls=%fused_computation.17 | convolution fusion | flops 6450315264 | bytes 16252928 | tf_op jit(solution)/shard_map/dot_general | solution.py:119
  505.2 8.6 %copy.35 = bf16[4096,768]{1,0:T(8,128)(2,1)} copy(bf16[4096,768]{0,1:T(8,128)(2,1)} %fusion.11) | data formatting | bytes 12582912
  513.8 0.0 reduce-scatter.4.cloned.1.call-update
  513.9 138.7 %all-reduce.2.cloned.1.call-done = bf16[1024,4096]{1,0:T(8,128)(2,1)} async-done(((bf16[1024,4096]{1,0:T(8,128)(2,1)}), bf16[1024,4096]{1,0:T(8,128)(2,1)}) %all-reduce.2.cloned.1.call-update) | async-done | bytes 8388624 | tf_op jit(solution)/shard_map/psum | solution.py:113
  652.6 3.1 convert_convert_fusion
  655.7 173.1 %reduce-scatter.4.cloned.1.call-done = bf16[128,768]{1,0:T(8,128)(2,1)} async-done(((bf16[4096,768]{1,0:T(8,128)(2,1)}), bf16[128,768]{1,0:T(8,128)(2,1)}) %reduce-scatter.4.cloned.1.call-update) | async-done | bytes 196624
  828.8 1.6 slice.15
  830.3 1.4 fusion.42
  (38 shorter events, 0.2 us)
Async XLA Ops:
  7.2 156.8 %all-gather.4.cloned.1.call-start = ((), (), s32[]{:S(2)}) async-start(), calls=%async_computation.2 | async-start | bytes 1081344 | tf_op jit(solution)/shard_map/all_gather | solution.py:95
  7.9 315.9 %all-gather.6.cloned.1.call-start = ((), (), s32[]{:S(2)}) async-start(), calls=%async_computation.3 | async-start | bytes 4325376 | tf_op jit(solution)/shard_map/all_gather | solution.py:94
  10.6 335.7 %all-to-all-start = ((bf16[32,128,128]{2,1,0:T(8,128)(2,1)}), bf16[32,128,128]{2,1,0:T(8,128)(2,1)}, u32[]{:S(2)}, u32[]{:S(2)}) async-start(bf16[32,128,128]{2,1,0:T(8,128)(2,1)} %stack.2), calls=%async_computation | async-start | bytes 2097152 | tf_op jit(solution)/shard_map/all_to_all | solution.py:97
  19.5 456.9 %all-gather.8.cloned.1.call-start = ((), (), s32[]{:S(2)}) async-start(), calls=%async_computation.4 | async-start | bytes 1081344 | tf_op jit(solution)/shard_map/all_gather | solution.py:107
  20.2 632.4 %all-reduce.2.cloned.1.call-start = ((), (), s32[]{:S(2)}) async-start(), calls=%async_computation.5 | async-start | bytes 16777216 | tf_op jit(solution)/shard_map/psum | solution.py:113
  21.6 148.9 %copy-start.10 = (f32[1024,64]{0,1:T(8,128)}, f32[1024,64]{0,1:T(8,128)S(1)}, u32[]{:S(2)}) copy-start(f32[1024,64]{0,1:T(8,128)S(1)} %get-tuple-element.25) | copy-start | bytes 786436
  323.8 8.5 %copy-start.5 = (f32[1024,128]{0,1:T(8,128)S(1)}, f32[1024,128]{0,1:T(8,128)}, u32[]{:S(2)}) copy-start(f32[1024,128]{0,1:T(8,128)} %get-tuple-element.22) | copy-start | bytes 1572868
  332.1 1.0 copy-start.3
  332.1 1.7 copy-start.8
  332.5 1.3 copy-start.1
  336.9 5.8 copy-start
  364.7 13.2 %copy-start.2 = (f32[1024,4,128]{0,2,1:T(8,128)S(1)}, f32[1024,4,128]{0,2,1:T(8,128)}, u32[]{:S(2)}) copy-start(f32[1024,4,128]{0,2,1:T(8,128)} %copy-done.1) | copy-start | bytes 6291460
  364.7 13.2 %copy-start.4 = (f32[1024,128]{0,1:T(8,128)S(1)}, f32[1024,128]{0,1:T(8,128)}, u32[]{:S(2)}) copy-start(f32[1024,128]{0,1:T(8,128)} %get-tuple-element.20) | copy-start | bytes 1572868
  378.0 3.0 copy-start.6
  378.0 3.0 copy-start.9
  382.4 1.2 copy-start.11
  382.4 1.4 copy-start.7
  383.7 9.5 %copy-start.13 = (bf16[4096,512]{1,0:T(8,128)(2,1)S(1)}, bf16[4096,512]{1,0:T(8,128)(2,1)}, u32[]{:S(2)}) copy-start(bf16[4096,512]{1,0:T(8,128)(2,1)} %all-gather.6.cloned.1.call-done) | copy-start | bytes 12582916
  383.7 17.9 %slice-start = ((s8[16777216]{0:T(1024)(128)(4,1)}), s8[4194304]{0:T(1024)(128)(4,1)S(1)}, s32[]{:S(2)}) async-start(s8[16777216]{0:T(1024)(128)(4,1)} %bitcast.129), calls=%async_computation.7 | async-start | bytes 8388608
  383.7 17.8 %slice-start.1 = ((s8[16777216]{0:T(1024)(128)(4,1)}), s8[4194304]{0:T(1024)(128)(4,1)S(1)}, s32[]{:S(2)}) async-start(s8[16777216]{0:T(1024)(128)(4,1)} %bitcast.129), calls=%async_computation.8 | async-start | bytes 8388608
  393.2 8.4 %slice-start.2 = ((s8[16777216]{0:T(1024)(128)(4,1)}), s8[4194304]{0:T(1024)(128)(4,1)S(1)}, s32[]{:S(2)}) async-start(s8[16777216]{0:T(1024)(128)(4,1)} %bitcast.129), calls=%async_computation.9 | async-start | bytes 8388608
  393.2 8.4 %slice-start.3 = ((s8[16777216]{0:T(1024)(128)(4,1)}), s8[4194304]{0:T(1024)(128)(4,1)S(1)}, s32[]{:S(2)}) async-start(s8[16777216]{0:T(1024)(128)(4,1)} %bitcast.129), calls=%async_computation.10 | async-start | bytes 8388608
  393.2 8.4 %copy-start.12 = (bf16[1024,512]{0,1:T(8,128)(2,1)S(1)}, bf16[1024,512]{0,1:T(8,128)(2,1)}, u32[]{:S(2)}) copy-start(bf16[1024,512]{0,1:T(8,128)(2,1)} %copy.40) | copy-start | bytes 3145732
  492.1 336.7 %reduce-scatter.4.cloned.1.call-start = ((), (), s32[]{:S(2)}) async-start(), calls=%async_computation.6 | async-start | bytes 6488064
Sparse Core Ops, SparseCore 0:
  9.6 154.2 all-gather.3
  165.6 158.1 all-gather.5
  325.4 150.9 all-gather.7
  492.2 160.3 all-reduce.1
  654.9 173.8 reduce-scatter.3
